TPU v7x, 512 devices: a whole 4x4x16 slice. The times are simulated.
512 devices in a mesh: dp: 64 (over z, x_lo, core), slab: 8 (over y, x_hi).
Axes of the slice: x: 4 (x_hi: 2, x_lo: 2; x = x_hi * 2 + x_lo), y: 4, z: 16, core: 2. Of those that a mesh axis runs over, the one named last changes fastest.
Arguments:
- voxels: bfloat16 [64, 8, 12, 32, 128], P('dp', None, None, 'slab'), may hold values from -16 to 16
- occupancy: int32 [64, 8, 12, 32], P('dp', None, None, 'slab'), may hold values 0 or 1
- out_grad: bfloat16 [64, 8, 12, 32, 128], P('dp', None, None, 'slab'), may hold values from -192 to 192
- weights: bfloat16 [2, 3456, 128], replicated, may hold values from -5 to 5
- master: float32 [2, 3456, 128], P(None, 'dp', 'slab'), may hold values from -5 to 5
- moment: float32 [2, 3456, 128], P(None, 'dp', 'slab'), may hold values from -18 to 18
- second: float32 [2, 3456, 128], P(None, 'dp', 'slab'), may hold values from 1 to 10
- teacher: float32 [2, 3456, 128], P(None, 'dp', 'slab'), may hold values from -5 to 5
Outputs:
- new_master: float32 [2, 3456, 128], P(None, 'dp', 'slab')
- new_moment: float32 [2, 3456, 128], P(None, 'dp', 'slab')
- new_second: float32 [2, 3456, 128], P(None, 'dp', 'slab')
- new_teacher: float32 [2, 3456, 128], P(None, 'dp', 'slab')
- new_weights: bfloat16 [2, 3456, 128], P(None, None, 'slab')
All inputs are finite; a program needn't handle non-finite values. No bound on the sum of `occupancy` on one device may be relied on, other than what follows from the above.
Results may differ from a plain program's by a relative error of at most 0.0013.
Values may be sent and summed in bfloat16 or wider, within the bound.
No kernel may reach another device: no remote copies, remote signals or barrier semaphores. Data moves between devices by JAX's collectives and lax.ppermute only.
A program may use at most 64 MiB of HBM per device.

v0:
```python
import jax
import jax.numpy as jnp
from jax import lax
from jax.sharding import PartitionSpec as P

C = 128
TAPS = 27
STEP_COUNT = 10
beta_first = 0.9
beta_second = 0.999
learning_rate = 0.01
weight_decay = 0.05
teacher_keep = 0.99
adam_epsilon = 1e-08


def with_halo(cells, sides, width):
    for axis, dim in sides:
        count = lax.axis_size(axis)
        ends = count - 1
        head = lax.slice_in_dim(cells, 0, width, axis=dim)
        tail = lax.slice_in_dim(cells, cells.shape[dim] - width, cells.shape[dim], axis=dim)
        cells = jnp.concatenate(
            [
                lax.ppermute(tail, axis, [(i, (i + 1) % count) for i in range(ends)]),
                cells,
                lax.ppermute(head, axis, [((i + 1) % count, i) for i in range(ends)]),
            ],
            axis=dim,
        )
    return cells


def tap_corners():
    return [
        (along_x, along_y, along_z)
        for along_x in range(3)
        for along_y in range(3)
        for along_z in range(3)
    ]


def unit_scale():
    return (TAPS * C) ** (-0.5)


def silu_slope(values):
    logistic = jax.nn.sigmoid(values)
    return logistic * (1.0 + values * (1.0 - logistic))


def take_window(padded, start, extent):
    window = padded[
        start[0] : start[0] + extent[0],
        start[1] : start[1] + extent[1],
        start[2] : start[2] + extent[2],
    ]
    return window.reshape(-1, window.shape[-1])


def forward_conv(padded, weight_rows, extent):
    channels = weight_rows.shape[1]
    summed = jnp.zeros((extent[0] * extent[1] * extent[2], channels), jnp.float32)
    for tap_index, corner in enumerate(tap_corners()):
        window = take_window(padded, corner, extent)
        block = weight_rows[tap_index * channels : (tap_index + 1) * channels]
        summed = summed + jnp.dot(window, block, preferred_element_type=jnp.float32)
    return (summed * unit_scale()).reshape(extent + (channels,))


def transposed_conv(padded_grad, weight_rows, extent):
    channels = weight_rows.shape[1]
    summed = jnp.zeros((extent[0] * extent[1] * extent[2], channels), jnp.float32)
    for tap_index, corner in enumerate(tap_corners()):
        start = (2 - corner[0], 2 - corner[1], 2 - corner[2])
        window = take_window(padded_grad, start, extent)
        block = weight_rows[tap_index * channels : (tap_index + 1) * channels]
        summed = summed + lax.dot_general(
            window, block, (((1,), (1,)), ((), ())), preferred_element_type=jnp.float32
        )
    return (summed * unit_scale()).reshape(extent + (channels,))


def weight_grad(padded, grad_field, extent):
    grad_rows = grad_field.reshape(-1, grad_field.shape[-1])
    blocks = []
    for corner in tap_corners():
        window = take_window(padded, corner, extent)
        blocks.append(
            lax.dot_general(
                window, grad_rows, (((0,), (0,)), ((), ())), preferred_element_type=jnp.float32
            )
        )
    return jnp.concatenate(blocks, axis=0) * unit_scale()


def adam_update(master, moment, second, teacher, gradient):
    new_moment = beta_first * moment + (1.0 - beta_first) * gradient
    new_second = beta_second * second + (1.0 - beta_second) * gradient * gradient
    first_fix = 1.0 - beta_first**STEP_COUNT
    second_fix = 1.0 - beta_second**STEP_COUNT
    ratio = new_moment / first_fix / (jnp.sqrt(new_second / second_fix) + adam_epsilon)
    new_master = master - learning_rate * (ratio + weight_decay * master)
    new_teacher = teacher_keep * teacher + (1.0 - teacher_keep) * new_master
    return (new_master, new_moment, new_second, new_teacher)


def local(voxels, occupancy, out_grad, weights, master, moment, second, teacher):
    own_cells = voxels[0]
    extent = tuple(own_cells.shape[:3])
    occupied = occupancy[0].astype(jnp.float32)[..., None]
    plane_pad = ((1, 1), (1, 1), (0, 0), (0, 0))
    rim_input = with_halo(own_cells, (("slab", 2),), 1)
    padded_in = jnp.pad(rim_input, plane_pad)
    pre_one = forward_conv(padded_in, weights[0], extent)
    act_one = (occupied * jax.nn.silu(pre_one)).astype(jnp.bfloat16)
    rim_hidden = with_halo(act_one, (("slab", 2),), 1)
    padded_act = jnp.pad(rim_hidden, plane_pad)
    pre_two = forward_conv(padded_act, weights[1], extent)
    grad_two = (out_grad[0].astype(jnp.float32) * occupied * silu_slope(pre_two)).astype(
        jnp.bfloat16
    )
    rim_grad = with_halo(grad_two, (("slab", 2),), 1)
    padded_grad = jnp.pad(rim_grad, plane_pad)
    wgrad_two = weight_grad(padded_act, grad_two, extent)
    back_one = transposed_conv(padded_grad, weights[1], extent)
    grad_one = (back_one * occupied * silu_slope(pre_one)).astype(jnp.bfloat16)
    wgrad_one = weight_grad(padded_in, grad_one, extent)
    weight_grads = jnp.stack([wgrad_one, wgrad_two])
    row_sums = lax.psum_scatter(weight_grads, "dp", scatter_dimension=1, tiled=True)
    gradient = lax.psum_scatter(row_sums, "slab", scatter_dimension=2, tiled=True)
    new_master, new_moment, new_second, new_teacher = adam_update(
        master, moment, second, teacher, gradient
    )
    fresh_weights = new_master.astype(jnp.bfloat16)
    new_weights = lax.all_gather(fresh_weights, "dp", axis=1, tiled=True)
    return (new_master, new_moment, new_second, new_teacher, new_weights)


def solution(mesh):
    in_specs = (
        P("dp", None, None, "slab", None),
        P("dp", None, None, "slab"),
        P("dp", None, None, "slab", None),
        P(),
        P(None, "dp", "slab"),
        P(None, "dp", "slab"),
        P(None, "dp", "slab"),
        P(None, "dp", "slab"),
    )
    out_specs = (
        P(None, "dp", "slab"),
        P(None, "dp", "slab"),
        P(None, "dp", "slab"),
        P(None, "dp", "slab"),
        P(None, None, "slab"),
    )
    return jax.shard_map(local, mesh=mesh, in_specs=in_specs, out_specs=out_specs, check_vma=False)
```

profile of v0, /device:TPU:1, one launch (start us, length us, event | category | flops | bytes accessed | tf_op | source)
XLA Modules:
  0.0 662.1 jit_solution(6944818351448994479)
XLA Ops:
  7.2 0.9 copy.675
  8.1 5.5 collective-permute-start
  13.6 1.3 collective-permute-start.1
  14.9 0.9 copy_convert_fusion
  15.9 0.7 fusion.352
  16.9 2.9 collective-permute-done.1
  20.0 0.6 fusion.347
  21.9 0.8 copy-done
  27.4 4.0 collective-permute-start.2
  31.4 1.3 collective-permute-start.3
  32.8 4.7 collective-permute-done.3
  37.7 0.3 fusion.345
  44.3 4.6 collective-permute-start.4
  48.9 1.5 collective-permute-start.5
  70.5 14.0 %copy.534 = f32[2,3456,128]{2,0,1:T(2,128)} copy(f32[2,3456,128]{2,1,0:T(8,128)S(1)} %pad_maximum_fusion) | data formatting | bytes 7077888 | tf_op jit(solution)/shard_map/stack | solution.py:129
  84.5 1.3 dynamic-slice
  85.8 1.3 dynamic-slice.2
  88.4 449.9 %all-reduce.7.cloned.1.call-done = f32[2,3456,128]{2,0,1:T(2,128)} async-done(((f32[2,3456,128]{2,0,1:T(2,128)}), f32[2,3456,128]{2,0,1:T(2,128)}) %all-reduce.7.cloned.1.call-update) | async-done | bytes 3538960
  538.3 0.8 constant_dynamic-slice_fusion.1
  539.2 36.3 %all-reduce.4 = f32[2,54,128]{1,0,2:T(2,128)S(1)} all-reduce(f32[2,54,128]{1,0,2:T(2,128)S(1)} %copy.535), channel_id=3, replica_groups=mesh['dp'=64,'slab'=8] {'slab'}, use_global_device_ids=true, to_apply=%region_1.2.clone | all-reduce | flops 13824 | bytes 110592
  575.6 0.6 fusion.341
  576.4 75.2 %all_gather.3 = bf16[2,3456,16]{2,0,1:T(2,128)(2,1)S(1)} all-gather(bf16[2,54,16]{2,0,1:T(2,128)(2,1)S(1)} %copy.539), channel_id=1, replica_groups=mesh['dp'=64,'slab'=8] {'dp'}, dimensions={1}, use_global_device_ids=true | all-gather | bytes 224640 | tf_op jit(solution)/shard_map/all_gather | solution.py:136
  651.6 3.0 copy.540
  654.6 0.6 multiply_add_fusion
  (261 shorter events, 32.1 us)
Async XLA Ops:
  7.2 531.1 %all-reduce.7.cloned.1.call-start = ((), (), s32[]{:S(2)}) async-start(), calls=%async_computation | async-start | bytes 7077888
  8.1 8.8 %collective-permute-start = (bf16[8,12,1,128]{3,1,2,0:T(8,128)(2,1)S(1)}, bf16[8,12,1,128]{3,1,2,0:T(8,128)(2,1)S(1)}, u32[]{:S(2)}, u32[]{:S(2)}) collective-permute-start(bf16[8,12,1,128]{3,1,2,0:T(8,128)(2,1)S(1)} %get-tuple-element.110), channel_id=1, source_target_pairs={{0,1},{1,2},{2,3},{3,4},{4,5},{5,6},{6,7},{8,9},{9,10},{10,11},{11... | collective-permute-start | bytes 73736 | tf_op jit(solution)/shard_map/ppermute | solution.py:25
  13.6 6.2 collective-permute-start.1
  21.1 1.5 copy-start
  23.6 1.2 copy-start.1
  27.4 5.4 collective-permute-start.2
  31.4 6.1 collective-permute-start.3
  42.7 1.2 copy-start.2
  44.3 12.4 %collective-permute-start.4 = (bf16[8,12,1,128]{3,0,2,1:T(8,128)(2,1)S(1)}, bf16[8,12,1,128]{3,0,2,1:T(8,128)(2,1)S(1)}, u32[]{:S(2)}, u32[]{:S(2)}) collective-permute-start(bf16[8,12,1,128]{3,0,2,1:T(8,128)(2,1)S(1)} %get-tuple-element.114), channel_id=1, source_target_pairs={{0,1},{1,2},{2,3},{3,4},{4,5},{5,6},{6,7},{8,9},{9,10},{10,11},{11... | collective-permute-start | bytes 73736 | tf_op jit(solution)/shard_map/ppermute | solution.py:25
  48.9 7.7 %collective-permute-start.5 = (bf16[8,12,1,128]{3,0,2,1:T(8,128)(2,1)S(1)}, bf16[8,12,1,128]{3,0,2,1:T(8,128)(2,1)S(1)}, u32[]{:S(2)}, u32[]{:S(2)}) collective-permute-start(bf16[8,12,1,128]{3,0,2,1:T(8,128)(2,1)S(1)} %get-tuple-element.115), channel_id=1, source_target_pairs={{1,0},{2,1},{3,2},{4,3},{5,4},{6,5},{7,6},{9,8},{10,9},{11,10},{12... | collective-permute-start | bytes 73736 | tf_op jit(solution)/shard_map/ppermute | solution.py:27
  84.5 491.1 %copy-start.4 = (f32[2,54,16]{1,2,0:T(8,128)S(1)}, f32[2,54,16]{1,2,0:T(8,128)}, u32[]{:S(2)}) copy-start(f32[2,54,16]{1,2,0:T(8,128)} %param.12) | copy-start | bytes 20740
  84.5 491.1 %copy-start.5 = (f32[2,54,16]{1,2,0:T(8,128)S(1)}, f32[2,54,16]{1,2,0:T(8,128)}, u32[]{:S(2)}) copy-start(f32[2,54,16]{1,2,0:T(8,128)} %param.13) | copy-start | bytes 20740
  84.5 491.1 %copy-start.6 = (f32[2,54,16]{1,2,0:T(8,128)S(1)}, f32[2,54,16]{1,2,0:T(8,128)}, u32[]{:S(2)}) copy-start(f32[2,54,16]{1,2,0:T(8,128)} %param.14) | copy-start | bytes 20740
  576.2 78.3 %copy-start.3 = (f32[2,54,16]{1,2,0:T(8,128)}, f32[2,54,16]{1,2,0:T(8,128)S(1)}, u32[]{:S(2)}) copy-start(f32[2,54,16]{1,2,0:T(8,128)S(1)} %get-tuple-element.31) | copy-start | bytes 20740
  576.4 78.2 %copy-start.7 = (f32[2,54,16]{1,2,0:T(8,128)S(1)}, f32[2,54,16]{1,2,0:T(8,128)}, u32[]{:S(2)}) copy-start(f32[2,54,16]{1,2,0:T(8,128)} %param.15) | copy-start | bytes 20740
Sparse Core Ops, SparseCore 0:
  84.6 453.6 all-reduce.6
where the time goes:
time: 663 us; the launch traced here: 662 us
  waiting for transfers between devices  458 us (69%)
  blocking collectives  112 us (17%)
  local copies, waits for them, and re-layouts  27.2 us (4%)
  matrix products  26.2 us (4%)
  starting transfers between devices  18.3 us (3%)
  between operations  16.9 us (3%)
    unnamed x2, waiting for transfers between devices  450 us
    all_gather x1, blocking collectives, local(): new_weights = lax.all_gather(fresh_weights, 'dp', axis=1, tiled=True)  75.2 us
    unnamed x1, blocking collectives  36.3 us
    ppermute x3, starting transfers between devices, with_halo(): lax.ppermute(tail, axis, [(i, (i + 1) % count) for i in range(ends)])  14.2 us
    another operation x1, local copies, waits for them, and re-layouts, local(): weight_grads = jnp.stack([wgrad_one, wgrad_two])  14 us
  transfers between devices with their start and end apart: 7, of which 3 were waited for; matrix products, arithmetic and copies ran while one was open for 2% of the time, Pallas kernels for 0%

commit v1 on v0

--- a/solution.py
+++ b/solution.py
@@ -12,6 +12,18 @@
 weight_decay = 0.05
 teacher_keep = 0.99
 adam_epsilon = 1e-08
+
+
+def _store_teams(arr, axis_name):
+    return jnp.concatenate(
+        lax.all_to_all(
+            jnp.stack(tuple((arr for _ in range(lax.axis_size(axis_name))))),
+            axis_name=axis_name,
+            split_axis=0,
+            concat_axis=0,
+        ),
+        axis=1,
+    )
 
 
 def with_halo(cells, sides, width):
@@ -133,7 +145,7 @@
         master, moment, second, teacher, gradient
     )
     fresh_weights = new_master.astype(jnp.bfloat16)
-    new_weights = lax.all_gather(fresh_weights, "dp", axis=1, tiled=True)
+    new_weights = _store_teams(fresh_weights, "dp")
     return (new_master, new_moment, new_second, new_teacher, new_weights)
 
 

time: 663 us -> 630 us (0.950)
  blocking collectives: 112 us -> 36.3 us
  starting transfers between devices: 18.3 us -> 39.1 us
  waiting for transfers between devices: 458 us -> 478 us
    all_gather x1 -> x0, blocking collectives: 75.2 us -> none  [local(): new_weights = lax.all_gather(fresh_weights, 'dp', axis=1, tiled=True)]
    all_to_all x0 -> x1, starting transfers between devices: none -> 20.9 us  [_store_teams(): lax.all_to_all(jnp.stack(tuple((arr for _ in range(lax.axis_size(axis_nam...]
    all_to_all x0 -> x1, waiting for transfers between devices: none -> 20.3 us  [_store_teams(): lax.all_to_all(jnp.stack(tuple((arr for _ in range(lax.axis_size(axis_nam...]
  transfers between devices with their start and end apart: 7 -> 8, of which waited for: 3 -> 4; matrix products, arithmetic and copies ran while one was open for 2% -> 2% of each run, Pallas kernels for 0% -> 0%
where the time goes in v1:
time: 630 us; the launch traced here: 629 us
  waiting for transfers between devices  478 us (76%)
  starting transfers between devices  39.1 us (6%)
  blocking collectives  36.3 us (6%)
  local copies, waits for them, and re-layouts  28.1 us (4%)
  matrix products  26.2 us (4%)
  between operations  17 us (3%)
    unnamed x2, waiting for transfers between devices  450 us
    unnamed x1, blocking collectives  36.3 us
    all_to_all x1, starting transfers between devices, _store_teams(): lax.all_to_all(jnp.stack(tuple((arr for _ in range(lax.axis_size(axis_nam...  20.9 us
    all_to_all x1, waiting for transfers between devices, _store_teams(): lax.all_to_all(jnp.stack(tuple((arr for _ in range(lax.axis_size(axis_nam...  20.3 us
    ppermute x3, starting transfers between devices, with_halo(): lax.ppermute(tail, axis, [(i, (i + 1) % count) for i in range(ends)])  14.2 us
    another operation x1, local copies, waits for them, and re-layouts, local(): weight_grads = jnp.stack([wgrad_one, wgrad_two])  13.9 us
  transfers between devices with their start and end apart: 8, of which 4 were waited for; matrix products, arithmetic and copies ran while one was open for 2% of the time, Pallas kernels for 0%

profile of v1, /device:TPU:1, one launch (start us, length us, event | category | flops | bytes accessed | tf_op | source)
XLA Modules:
  0.0 629.0 jit_solution(5979622858788280141)
XLA Ops:
  7.2 0.9 copy.673
  8.1 5.5 collective-permute-start
  13.6 1.3 collective-permute-start.1
  14.9 0.9 copy_convert_fusion
  15.9 0.7 fusion.352
  16.9 2.9 collective-permute-done.1
  21.7 0.8 copy-done
  27.2 4.0 collective-permute-start.2
  31.3 1.3 collective-permute-start.3
  32.7 4.7 collective-permute-done.3
  44.1 4.6 collective-permute-start.4
  48.8 1.5 collective-permute-start.5
  70.4 13.9 %copy.533 = f32[2,3456,128]{2,0,1:T(2,128)} copy(f32[2,3456,128]{2,1,0:T(8,128)S(1)} %pad_maximum_fusion) | data formatting | bytes 7077888 | tf_op jit(solution)/shard_map/stack | solution.py:141
  84.4 1.3 dynamic-slice
  85.7 1.3 dynamic-slice.2
  88.3 449.9 %all-reduce.7.cloned.1.call-done = f32[2,3456,128]{2,0,1:T(2,128)} async-done(((f32[2,3456,128]{2,0,1:T(2,128)}), f32[2,3456,128]{2,0,1:T(2,128)}) %all-reduce.7.cloned.1.call-update) | async-done | bytes 3538960
  538.1 0.8 constant_dynamic-slice_fusion.1
  539.1 36.3 %all-reduce.4 = f32[2,54,128]{1,0,2:T(2,128)S(1)} all-reduce(f32[2,54,128]{1,0,2:T(2,128)S(1)} %copy.534), channel_id=3, replica_groups=mesh['dp'=64,'slab'=8] {'slab'}, use_global_device_ids=true, to_apply=%region_1.2.clone | all-reduce | flops 13824 | bytes 110592
  575.5 0.6 fusion.341
  576.2 1.6 reshape.1275
  577.8 20.9 %all-to-all-start = ((bf16[64,2,864]{2,1,0:T(2,128)(2,1)}), bf16[64,2,864]{2,1,0:T(2,128)(2,1)S(1)}, u32[]{:S(2)}, u32[]{:S(2)}) async-start(bf16[64,2,864]{2,1,0:T(2,128)(2,1)} %reshape.1275), calls=%async_computation | async-start | bytes 458752 | tf_op jit(solution)/shard_map/all_to_all | solution.py:19
  599.3 20.3 %all-to-all-done = bf16[64,2,864]{2,1,0:T(2,128)(2,1)S(1)} async-done(((bf16[64,2,864]{2,1,0:T(2,128)(2,1)}), bf16[64,2,864]{2,1,0:T(2,128)(2,1)S(1)}, u32[]{:S(2)}, u32[]{:S(2)}) %all-to-all-start) | async-done | bytes 221216 | tf_op jit(solution)/shard_map/all_to_all | solution.py:19
  619.6 0.9 reshape.1276
  620.8 1.4 reshape.1216
  (266 shorter events, 33.7 us)
Async XLA Ops:
  7.2 531.0 %all-reduce.7.cloned.1.call-start = ((), (), s32[]{:S(2)}) async-start(), calls=%async_computation.1 | async-start | bytes 7077888
  8.1 8.8 %collective-permute-start = (bf16[8,12,1,128]{3,1,2,0:T(8,128)(2,1)S(1)}, bf16[8,12,1,128]{3,1,2,0:T(8,128)(2,1)S(1)}, u32[]{:S(2)}, u32[]{:S(2)}) collective-permute-start(bf16[8,12,1,128]{3,1,2,0:T(8,128)(2,1)S(1)} %get-tuple-element.100), channel_id=1, source_target_pairs={{0,1},{1,2},{2,3},{3,4},{4,5},{5,6},{6,7},{8,9},{9,10},{10,11},{11... | collective-permute-start | bytes 73736 | tf_op jit(solution)/shard_map/ppermute | solution.py:37
  13.6 6.2 collective-permute-start.1
  21.0 1.5 copy-start
  23.5 1.2 copy-start.1
  27.2 5.4 collective-permute-start.2
  31.3 6.1 collective-permute-start.3
  42.5 1.2 copy-start.2
  44.1 12.4 %collective-permute-start.4 = (bf16[8,12,1,128]{3,0,2,1:T(8,128)(2,1)S(1)}, bf16[8,12,1,128]{3,0,2,1:T(8,128)(2,1)S(1)}, u32[]{:S(2)}, u32[]{:S(2)}) collective-permute-start(bf16[8,12,1,128]{3,0,2,1:T(8,128)(2,1)S(1)} %get-tuple-element.104), channel_id=1, source_target_pairs={{0,1},{1,2},{2,3},{3,4},{4,5},{5,6},{6,7},{8,9},{9,10},{10,11},{11... | collective-permute-start | bytes 73736 | tf_op jit(solution)/shard_map/ppermute | solution.py:37
  48.8 7.7 %collective-permute-start.5 = (bf16[8,12,1,128]{3,0,2,1:T(8,128)(2,1)S(1)}, bf16[8,12,1,128]{3,0,2,1:T(8,128)(2,1)S(1)}, u32[]{:S(2)}, u32[]{:S(2)}) collective-permute-start(bf16[8,12,1,128]{3,0,2,1:T(8,128)(2,1)S(1)} %get-tuple-element.105), channel_id=1, source_target_pairs={{1,0},{2,1},{3,2},{4,3},{5,4},{6,5},{7,6},{9,8},{10,9},{11,10},{12... | collective-permute-start | bytes 73736 | tf_op jit(solution)/shard_map/ppermute | solution.py:39
  84.4 491.1 %copy-start.4 = (f32[2,54,16]{1,2,0:T(8,128)S(1)}, f32[2,54,16]{1,2,0:T(8,128)}, u32[]{:S(2)}) copy-start(f32[2,54,16]{1,2,0:T(8,128)} %param.12) | copy-start | bytes 20740
  84.4 491.1 %copy-start.5 = (f32[2,54,16]{1,2,0:T(8,128)S(1)}, f32[2,54,16]{1,2,0:T(8,128)}, u32[]{:S(2)}) copy-start(f32[2,54,16]{1,2,0:T(8,128)} %param.13) | copy-start | bytes 20740
  84.4 491.1 %copy-start.6 = (f32[2,54,16]{1,2,0:T(8,128)S(1)}, f32[2,54,16]{1,2,0:T(8,128)}, u32[]{:S(2)}) copy-start(f32[2,54,16]{1,2,0:T(8,128)} %param.14) | copy-start | bytes 20740
  84.4 514.3 %copy-start.7 = (f32[2,54,16]{1,2,0:T(8,128)S(1)}, f32[2,54,16]{1,2,0:T(8,128)}, u32[]{:S(2)}) copy-start(f32[2,54,16]{1,2,0:T(8,128)} %param.15) | copy-start | bytes 20740
  576.1 44.4 %copy-start.3 = (f32[2,54,16]{1,2,0:T(8,128)}, f32[2,54,16]{1,2,0:T(8,128)S(1)}, u32[]{:S(2)}) copy-start(f32[2,54,16]{1,2,0:T(8,128)S(1)} %get-tuple-element.21) | copy-start | bytes 20740
  577.8 41.8 %all-to-all-start = ((bf16[64,2,864]{2,1,0:T(2,128)(2,1)}), bf16[64,2,864]{2,1,0:T(2,128)(2,1)S(1)}, u32[]{:S(2)}, u32[]{:S(2)}) async-start(bf16[64,2,864]{2,1,0:T(2,128)(2,1)} %reshape.1275), calls=%async_computation | async-start | bytes 458752 | tf_op jit(solution)/shard_map/all_to_all | solution.py:19
Sparse Core Ops, SparseCore 0:
  84.5 453.5 all-reduce.6
